TPU v7x, 256 devices: a whole 4x4x8 slice. The times are simulated.
256 devices in a mesh: rows: 128 (over x, y, z), help: 2 (over core).
Axes of the slice: x: 4, y: 4, z: 8, core: 2. Of those that a mesh axis runs over, the one named last changes fastest.
Arguments:
- density: float32 [256, 5, 256, 256], P('rows', None, None, 'help'), as said below
- pattern: int32 [256, 5], P('rows'), may hold values from 0 to 1, as said below
- truncation: int32 [2, 256, 5], P(None, 'rows'), may hold values from 0 to 1, as said below
Outputs:
- purified: float32 [256, 5, 256, 256], P('rows', None, None, 'help')
Inputs may be any that keep to these rules, and one draw needn't show every extreme that they name: pattern[i, 2] = 1; pattern[i, s] = pattern[i + s - 2, 4 - s]; pattern[i, s] = 0 where i + s - 2 lies outside 0 to 255. truncation[t] obeys the same three rules as pattern for every t. density is symmetric: tile slot s of block row i is the transpose of slot 4 - s of block row i + s - 2 wherever both lie inside the matrix.
All inputs are finite; a program needn't handle non-finite values.
Results may differ from a plain program's by a relative error of at most 0.0002.
Values sent between devices are 32-bit elements; how exact they have to be, the bound alone decides.
No kernel may reach another device: no remote copies, remote signals or barrier semaphores. Data moves between devices by JAX's collectives and lax.ppermute only.
A program may use at most 64 MiB of HBM per device.

v0:
```python
import functools

import jax
import jax.numpy as jnp
from jax import lax
from jax.experimental import pallas as pl
from jax.experimental.pallas import tpu as pltpu
from jax.sharding import PartitionSpec as P


DIAG = ((0, 2), (0, 3), (1, 1), (1, 2))
OFF = ((0, 0), (0, 1), (0, 4), (1, 0), (1, 3), (1, 4))
ALL = tuple((row, slot) for row in range(2) for slot in range(5))
CONTRACT = (((1,), (0,)), ((), ()))


def swap_help(value):
    return lax.ppermute(value, "help", [(0, 1), (1, 0)])


def send_block(block):
    count = lax.axis_size("rows")
    from_left = lax.ppermute(block, "rows", [(i, i + 1) for i in range(count - 1)])
    from_right = lax.ppermute(block, "rows", [(i + 1, i) for i in range(count - 1)])
    return from_left, from_right


def split(x):
    high = x.astype(jnp.bfloat16)
    return high, (x - high.astype(jnp.float32)).astype(jnp.bfloat16)


class Tiles:
    def __init__(self, refs, scale):
        self.refs = refs
        self.scale = scale

    def __call__(self, row, slot, rows=slice(None)):
        if len(self.refs) == 1:
            value = self.refs[0][row, slot, rows, :]
        elif (row, slot) in DIAG:
            value = self.refs[0][DIAG.index((row, slot)), rows, :]
        else:
            value = self.refs[1][OFF.index((row, slot)), rows, :]
        if self.scale is not None:
            value = value * self.scale[row, slot].astype(jnp.float32)
        return value


QUARTERS = ((0, 2), (0, 3), (1, 2))
FROM_QUARTER = {(0, 2): (0, False, (0, 2)), (0, 3): (1, False, (1, 1)), (1, 1): (1, True, (0, 3)), (1, 2): (2, False, (1, 2))}


class Rebuilt:
    def __init__(self, quarter_ref, off_ref, mine, side, own, far):
        self.quarter_ref, self.off_ref, self.mine = quarter_ref, off_ref, mine
        self.side, self.own, self.far = side, own, far

    def __call__(self, row, slot, rows=slice(None)):
        if (row, slot) not in DIAG:
            return self.off_ref[OFF.index((row, slot)), rows, :]
        index, flip, source = FROM_QUARTER[(row, slot)]
        quarter = self.quarter_ref[index]
        far_rows = quarter.T if flip else quarter
        own_rows = self.mine(source[0], source[1], self.far).T
        return jnp.where(
            self.side == 0,
            jnp.concatenate([own_rows, far_rows], axis=0),
            jnp.concatenate([far_rows, own_rows], axis=0),
        )


def band_kernel(tiles, odd, parts, scaled, mode, quarters, side_ref, scale_ref, keep_ref, *rest):
    mine = Tiles(rest[:parts], scale_ref if scaled else None)
    rest = rest[parts:]
    other_refs = rest[: len(rest) - 5 - (3 if mode == "halo" else (2 if mode == "plain" else 0)) - (1 if quarters else 0)]
    rest = rest[len(other_refs) :]
    if mode in ("plain", "halo"):
        left_ref, right_ref = rest[:2]
        rest = rest[2:]
    if mode == "halo":
        partial_ref = rest[0]
        rest = rest[1:]
    if quarters:
        out_ref, quarter_ref, lh_ref, ll_ref, rh_ref, rl_ref = rest
    else:
        out_ref, lh_ref, ll_ref, rh_ref, rl_ref = rest
    tile = lh_ref.shape[1]
    half = tile // 2
    side = side_ref[0]
    own = pl.ds(pl.multiple_of(side * half, half), half)
    far = pl.ds(pl.multiple_of((1 - side) * half, half), half)
    if other_refs[0].shape[-2] == half:
        other = Rebuilt(other_refs[0], other_refs[1] if len(other_refs) > 1 else None, mine, side, own, far)
    else:
        other = Tiles(other_refs, scale_ref if scaled else None)
    by_row = [[(index, slot) for index, (row, slot) in enumerate(tiles) if row == r] for r in range(2)]

    def wanted(k):
        if mode == "own":
            return k in (0, 1)
        if mode == "halo":
            return k not in (0, 1)
        return True

    for row in range(2):
        offsets = [o for o in range(5) if wanted(row + o - 2)]
        for place_k, offset in enumerate(offsets):
            high, low = split(jnp.concatenate([mine(row, offset), other(row, offset)], axis=1))
            lh_ref[row, :, place_k * tile : (place_k + 1) * tile] = high
            ll_ref[row, :, place_k * tile : (place_k + 1) * tile] = low
            k = row + offset - 2
            for place, (index, slot) in enumerate(by_row[row]):
                col = row + slot - 2
                where = (row, slice(place_k * tile, (place_k + 1) * tile), slice(place * half, (place + 1) * half))
                if abs(k - col) > 2:
                    rh_ref[where] = jnp.zeros((tile, half), jnp.bfloat16)
                    rl_ref[where] = jnp.zeros((tile, half), jnp.bfloat16)
                    continue
                if k in (0, 1):
                    b = col - k + 2
                    right = jnp.concatenate([mine(k, b, own), mine(k, b, far)], axis=0)
                elif col not in (0, 1):
                    src = left_ref if k < 0 else right_ref
                    b = 2 * (k + 2) + (col + 2) if k < 0 else 2 * (k - 2) + (col - 2)
                    right = jnp.concatenate([src[b, own, :], src[b, far, :]], axis=0)
                else:
                    s = k - col + 2
                    right = jnp.concatenate([mine(col, s, own), other(col, s, own)], axis=1).T
                high, low = split(right)
                rh_ref[where] = high
                rl_ref[where] = low

    def one(x, y):
        return lax.dot_general(x, y, CONTRACT, preferred_element_type=jnp.float32)

    for row in range(2):
        offsets = [o for o in range(5) if wanted(row + o - 2)]
        row_tiles = by_row[row]
        values = []
        for first in range(0, len(row_tiles), 2):
            chunk = range(first, min(first + 2, len(row_tiles)))
            used = [
                place_k
                for place_k, offset in enumerate(offsets)
                if any(abs(offset - row_tiles[place][1]) <= 2 for place in chunk)
            ]
            ks = slice(used[0] * tile, (used[-1] + 1) * tile)
            ns = slice(chunk[0] * half, (chunk[-1] + 1) * half)
            a_high = lh_ref[row, :, ks]
            b_high = rh_ref[row, ks, ns]
            acc = one(ll_ref[row, :, ks], b_high) + one(a_high, rl_ref[row, ks, ns]) + one(a_high, b_high)
            values += [acc[:, n * half : (n + 1) * half] for n in range(len(chunk))]
        for place, (index, slot) in enumerate(row_tiles):
            value = values[place]
            if mode == "own":
                out_ref[row, slot] = value
                continue
            if mode == "halo":
                value = value + partial_ref[row, slot]
            if odd:
                value = 2.0 * mine(row, slot) - value
            value = value * keep_ref[row, slot].astype(jnp.float32)
            if len(tiles) == len(ALL):
                out_ref[row, slot] = value
            else:
                out_ref[index] = value
    if quarters:
        for index, key in enumerate(QUARTERS):
            quarter_ref[index] = out_ref[tiles.index(key), own, :]


def band_call(tiles, odd, side, scale, keep, mine, other, halo=None, scaled=False, quarters=False, mode=None, partial=None):
    smem = pl.BlockSpec(memory_space=pltpu.SMEM)
    vmem = pl.BlockSpec(memory_space=pltpu.VMEM)
    if mode is None:
        mode = "plain" if halo is not None else "none"
    args = [side, scale, keep] + list(mine) + list(other)
    if halo is not None:
        args += list(halo)
    if partial is not None:
        args.append(partial)
    half = mine[0].shape[-1]
    tile = (mine[0].shape[-2], half)
    shape = (2, 5) + tile if len(tiles) == len(ALL) else (len(tiles),) + tile
    width = len(tiles) // 2
    count = {"own": 2, "halo": 3}.get(mode, 5)
    lefts = (2, tile[0], count * 2 * half)
    rights = (2, count * tile[0], width * half)
    out_shape = jax.ShapeDtypeStruct(shape, jnp.float32)
    if quarters:
        out_shape = (out_shape, jax.ShapeDtypeStruct((len(QUARTERS), half, half), jnp.float32))
    return pl.pallas_call(
        functools.partial(band_kernel, tiles, odd, len(mine), scaled, mode, quarters),
        out_shape=out_shape,
        in_specs=[smem, smem, smem] + [vmem] * (len(args) - 3),
        out_specs=(vmem, vmem) if quarters else vmem,
        scratch_shapes=[pltpu.VMEM(lefts, jnp.bfloat16)] * 2 + [pltpu.VMEM(rights, jnp.bfloat16)] * 2,
    )(*args)


def block_kernel(pattern_ref, density_ref, out_ref):
    for index, (row, slot) in enumerate(DIAG):
        out_ref[index] = density_ref[row, slot] * pattern_ref[row, slot].astype(jnp.float32)


def first_block(pattern, density):
    return pl.pallas_call(
        block_kernel,
        out_shape=jax.ShapeDtypeStruct((len(DIAG),) + density.shape[2:], jnp.float32),
        in_specs=[pl.BlockSpec(memory_space=pltpu.SMEM), pl.BlockSpec(memory_space=pltpu.VMEM)],
        out_specs=pl.BlockSpec(memory_space=pltpu.VMEM),
    )(pattern, density)


def purify(density, pattern, truncation):
    side = lax.axis_index("help").astype(jnp.int32).reshape(1)
    halo = send_block(first_block(pattern, density))
    other = swap_help(density)
    diag, quarter = band_call(DIAG, False, side, pattern, truncation[0], [density], [other], scaled=True, quarters=True)
    next_halo = send_block(diag)
    quarter_other = swap_help(quarter)
    off = band_call(OFF, False, side, pattern, truncation[0], [density], [other], halo, scaled=True)
    off_other = swap_help(off)
    partial = band_call(ALL, True, side, pattern, truncation[1], [diag, off], [quarter_other], mode="own")
    return band_call(
        ALL, True, side, pattern, truncation[1], [diag, off], [quarter_other, off_other], next_halo, mode="halo", partial=partial
    )


def solution(mesh):
    return jax.shard_map(
        purify,
        mesh=mesh,
        in_specs=(P("rows", None, None, "help"), P("rows", None), P(None, "rows", None)),
        out_specs=P("rows", None, None, "help"),
        check_vma=False,
    )
```

profile of v0, /device:TPU:6, one launch (start us, length us, event | category | flops | bytes accessed | tf_op | source)
XLA Modules:
  0.0 72.8 jit_solution(5278028297959151075)
XLA Ops:
  0.0 0.0 copy-start.7
  0.0 0.0 collective-permute-start
  0.0 2.2 %shard_map.38 = f32[4,256,128]{2,1,0:T(8,128)} custom-call(s32[2,5]{1,0:T(2,128)} %scale_ref.7, f32[2,5,256,128]{3,2,1,0:T(8,128)} %rest_0_.3), custom_call_target="tpu_custom_call" | custom-call | tf_op jit(solution)/shard_map/pallas_call | solution.py:208
  2.2 10.5 %collective-permute-start.2 = (f32[4,256,128]{2,1,0:T(8,128)}, f32[4,256,128]{2,1,0:T(8,128)S(1)}, u32[]{:S(2)}, u32[]{:S(2)}) collective-permute-start(f32[4,256,128]{2,1,0:T(8,128)} %shard_map.38), channel_id=1, source_target_pairs={{2,0},{4,2},{6,4},{8,6},{10,8},{12,10},{14,12},{16,14},{18,16},{20... | collective-permute-start | bytes 1572872 | tf_op jit(solution)/shard_map/ppermute | solution.py:24
  12.6 1.9 %collective-permute-start.1 = (f32[4,256,128]{2,1,0:T(8,128)}, f32[4,256,128]{2,1,0:T(8,128)S(1)}, u32[]{:S(2)}, u32[]{:S(2)}) collective-permute-start(f32[4,256,128]{2,1,0:T(8,128)} %shard_map.38), channel_id=1, source_target_pairs={{0,2},{2,4},{4,6},{6,8},{8,10},{10,12},{12,14},{14,16},{16,18},{18... | collective-permute-start | bytes 1572872 | tf_op jit(solution)/shard_map/ppermute | solution.py:23
  14.6 0.0 copy-done.7
  14.6 0.6 slice_bitcast_fusion
  15.2 9.6 %collective-permute-done.2.rest_3_ = f32[4,256,128]{2,1,0:T(8,128)S(1)} collective-permute-done((f32[4,256,128]{2,1,0:T(8,128)}, f32[4,256,128]{2,1,0:T(8,128)S(1)}, u32[]{:S(2)}, u32[]{:S(2)}) %collective-permute-start.2) | collective-permute-done | bytes 524320 | tf_op jit(solution)/shard_map/ppermute | solution.py:24
  24.8 0.0 copy-start.5
  24.8 8.2 %collective-permute-done.1.rest_2_ = f32[4,256,128]{2,1,0:T(8,128)S(1)} collective-permute-done((f32[4,256,128]{2,1,0:T(8,128)}, f32[4,256,128]{2,1,0:T(8,128)S(1)}, u32[]{:S(2)}, u32[]{:S(2)}) %collective-permute-start.1) | collective-permute-done | bytes 524320 | tf_op jit(solution)/shard_map/ppermute | solution.py:23
  33.0 0.0 copy-start.6
  33.0 0.0 collective-permute-done.rest_1_
  33.0 0.0 copy-start
  33.0 0.0 copy-done.5
  33.0 0.8 %copy-done.6 = f32[4,256,128]{2,1,0:T(8,128)} copy-done((f32[4,256,128]{2,1,0:T(8,128)}, f32[4,256,128]{2,1,0:T(8,128)S(1)}, u32[]{:S(2)}) %copy-start.6) | copy-done | bytes 524312
  33.8 0.4 copy-done
  34.2 4.9 %shard_map.39.rest_1_ = f32[6,256,128]{2,1,0:T(8,128)} custom-call(s32[1]{0:T(128)} %bitcast.side_ref, s32[2,5]{1,0:T(2,128)} %scale_ref.7, s32[2,5]{1,0:T(2,128)} %get-tuple-element.9.keep_ref, f32[2,5,256,128]{3,2,1,0:T(8,128)} %rest_0_.3, f32[2,5,256,128]{3,2,1,0:T(8,128)} %copy-done, f32[4,256,128]{2,1,0:T(8,128)} %copy-done.6, f32[4,256,128]{2,1,0:T(8,128)} %copy-done.5), custom_call_target="tpu_custom_call" | custom-call | tf_op jit(solution)/shard_map/pallas_call | solution.py:193
  39.2 0.0 collective-permute-start.4
  39.2 4.3 %shard_map.37 = (f32[4,256,128]{2,1,0:T(8,128)}, f32[3,128,128]{2,1,0:T(8,128)}) custom-call(s32[1]{0:T(128)} %bitcast.side_ref, s32[2,5]{1,0:T(2,128)} %scale_ref.7, s32[2,5]{1,0:T(2,128)} %get-tuple-element.9.keep_ref, f32[2,5,256,128]{3,2,1,0:T(8,128)} %rest_0_.3, f32[2,5,256,128]{3,2,1,0:T(8,128)} %copy-done), custom_call_target="tpu_custom_call" | custom-call | tf_op jit(solution)/shard_map/pallas_call | solution.py:193
  43.4 1.9 %collective-permute-start.6 = (f32[4,256,128]{2,1,0:T(8,128)}, f32[4,256,128]{2,1,0:T(8,128)S(1)}, u32[]{:S(2)}, u32[]{:S(2)}) collective-permute-start(f32[4,256,128]{2,1,0:T(8,128)} %get-tuple-element.7.rest_0_), channel_id=1, source_target_pairs={{2,0},{4,2},{6,4},{8,6},{10,8},{12,10},{14,12},{16,14},{18,16},{20... | collective-permute-start | bytes 1572872 | tf_op jit(solution)/shard_map/ppermute | solution.py:24
  45.4 3.9 %collective-permute-start.5 = (f32[4,256,128]{2,1,0:T(8,128)}, f32[4,256,128]{2,1,0:T(8,128)S(1)}, u32[]{:S(2)}, u32[]{:S(2)}) collective-permute-start(f32[4,256,128]{2,1,0:T(8,128)} %get-tuple-element.7.rest_0_), channel_id=1, source_target_pairs={{0,2},{2,4},{4,6},{6,8},{8,10},{10,12},{12,14},{14,16},{16,18},{18... | collective-permute-start | bytes 1572872 | tf_op jit(solution)/shard_map/ppermute | solution.py:23
  49.3 0.1 collective-permute-start.3
  49.4 1.6 %collective-permute-done.3.rest_2_ = f32[3,128,128]{2,1,0:T(8,128)S(1)} collective-permute-done((f32[3,128,128]{2,1,0:T(8,128)}, f32[3,128,128]{2,1,0:T(8,128)S(1)}, u32[]{:S(2)}, u32[]{:S(2)}) %collective-permute-start.3) | collective-permute-done | bytes 196640 | tf_op jit(solution)/shard_map/ppermute | solution.py:18
  51.0 0.7 copy-done.1
  51.7 3.8 %shard_map.40.rest_6_ = f32[2,5,256,128]{3,2,1,0:T(8,128)} custom-call(s32[1]{0:T(128)} %bitcast.side_ref, s32[2,5]{1,0:T(2,128)} %scale_ref.7, s32[2,5]{1,0:T(2,128)} %get-tuple-element.10.keep_ref, f32[4,256,128]{2,1,0:T(8,128)} %get-tuple-element.7.rest_0_, f32[6,256,128]{2,1,0:T(8,128)} %shard_map.39.rest_1_, f32[3,128,128]{2,1,0:T(8,128)} %copy-done.1), custom_call_target="tpu_custom_call" | custom-call | tf_op jit(solution)/shard_map/pallas_call | solution.py:193
  55.5 4.3 %collective-permute-done.6.rest_5_ = f32[4,256,128]{2,1,0:T(8,128)S(1)} collective-permute-done((f32[4,256,128]{2,1,0:T(8,128)}, f32[4,256,128]{2,1,0:T(8,128)S(1)}, u32[]{:S(2)}, u32[]{:S(2)}) %collective-permute-start.6) | collective-permute-done | bytes 524320 | tf_op jit(solution)/shard_map/ppermute | solution.py:24
  59.9 6.1 %collective-permute-done.5.rest_4_ = f32[4,256,128]{2,1,0:T(8,128)S(1)} collective-permute-done((f32[4,256,128]{2,1,0:T(8,128)}, f32[4,256,128]{2,1,0:T(8,128)S(1)}, u32[]{:S(2)}, u32[]{:S(2)}) %collective-permute-start.5) | collective-permute-done | bytes 524320 | tf_op jit(solution)/shard_map/ppermute | solution.py:23
  66.0 0.0 collective-permute-done.4.rest_3_
  66.0 0.0 copy-done.3
  66.0 0.8 %copy-done.4 = f32[4,256,128]{2,1,0:T(8,128)} copy-done((f32[4,256,128]{2,1,0:T(8,128)}, f32[4,256,128]{2,1,0:T(8,128)S(1)}, u32[]{:S(2)}) %copy-start.4) | copy-done | bytes 524312
  66.8 0.9 %copy-done.2 = f32[6,256,128]{2,1,0:T(8,128)} copy-done((f32[6,256,128]{2,1,0:T(8,128)}, f32[6,256,128]{2,1,0:T(8,128)S(1)}, u32[]{:S(2)}) %copy-start.2) | copy-done | bytes 786456
  67.7 5.1 %shard_map.41 = f32[2,5,256,128]{3,2,1,0:T(8,128)} custom-call(s32[1]{0:T(128)} %bitcast.side_ref, s32[2,5]{1,0:T(2,128)} %scale_ref.7, s32[2,5]{1,0:T(2,128)} %get-tuple-element.10.keep_ref, f32[4,256,128]{2,1,0:T(8,128)} %get-tuple-element.7.rest_0_, f32[6,256,128]{2,1,0:T(8,128)} %shard_map.39.rest_1_, f32[3,128,128]{2,1,0:T(8,128)} %copy-done.1, ...), custom_call_target="tpu_custom_call" | custom-call | tf_op jit(solution)/shard_map/pallas_call | solution.py:193
  (4 shorter events, 0.0 us)
Async XLA Ops:
  0.0 14.6 %copy-start.7 = (s32[2,2,5]{2,1,0:T(2,128)S(1)}, s32[2,2,5]{2,1,0:T(2,128)}, u32[]{:S(2)}) copy-start(s32[2,2,5]{2,1,0:T(2,128)} %param.5) | copy-start | bytes 244
  0.0 33.0 %collective-permute-start = (f32[2,5,256,128]{3,2,1,0:T(8,128)}, f32[2,5,256,128]{3,2,1,0:T(8,128)S(1)}, u32[]{:S(2)}, u32[]{:S(2)}) collective-permute-start(f32[2,5,256,128]{3,2,1,0:T(8,128)} %rest_0_.3), channel_id=1, source_target_pairs={{0,1},{1,0},{2,3},{3,2},{4,5},{5,4},{6,7},{7,6},{8,9},{9,8},{10,11... | collective-permute-start | bytes 3932168 | tf_op jit(solution)/shard_map/ppermute | solution.py:18
  2.2 22.6 %collective-permute-start.2 = (f32[4,256,128]{2,1,0:T(8,128)}, f32[4,256,128]{2,1,0:T(8,128)S(1)}, u32[]{:S(2)}, u32[]{:S(2)}) collective-permute-start(f32[4,256,128]{2,1,0:T(8,128)} %shard_map.38), channel_id=1, source_target_pairs={{2,0},{4,2},{6,4},{8,6},{10,8},{12,10},{14,12},{16,14},{18,16},{20... | collective-permute-start | bytes 1572872 | tf_op jit(solution)/shard_map/ppermute | solution.py:24
  12.6 20.4 %collective-permute-start.1 = (f32[4,256,128]{2,1,0:T(8,128)}, f32[4,256,128]{2,1,0:T(8,128)S(1)}, u32[]{:S(2)}, u32[]{:S(2)}) collective-permute-start(f32[4,256,128]{2,1,0:T(8,128)} %shard_map.38), channel_id=1, source_target_pairs={{0,2},{2,4},{4,6},{6,8},{8,10},{10,12},{12,14},{14,16},{16,18},{18... | collective-permute-start | bytes 1572872 | tf_op jit(solution)/shard_map/ppermute | solution.py:23
  24.8 8.2 %copy-start.5 = (f32[4,256,128]{2,1,0:T(8,128)}, f32[4,256,128]{2,1,0:T(8,128)S(1)}, u32[]{:S(2)}) copy-start(f32[4,256,128]{2,1,0:T(8,128)S(1)} %collective-permute-done.2.rest_3_) | copy-start | bytes 1572868
  33.0 0.8 %copy-start.6 = (f32[4,256,128]{2,1,0:T(8,128)}, f32[4,256,128]{2,1,0:T(8,128)S(1)}, u32[]{:S(2)}) copy-start(f32[4,256,128]{2,1,0:T(8,128)S(1)} %collective-permute-done.1.rest_2_) | copy-start | bytes 1572868
  33.0 1.2 %copy-start = (f32[2,5,256,128]{3,2,1,0:T(8,128)}, f32[2,5,256,128]{3,2,1,0:T(8,128)S(1)}, u32[]{:S(2)}) copy-start(f32[2,5,256,128]{3,2,1,0:T(8,128)S(1)} %collective-permute-done.rest_1_) | copy-start | bytes 3932164
  39.2 26.9 %collective-permute-start.4 = (f32[6,256,128]{2,1,0:T(8,128)}, f32[6,256,128]{2,1,0:T(8,128)S(1)}, u32[]{:S(2)}, u32[]{:S(2)}) collective-permute-start(f32[6,256,128]{2,1,0:T(8,128)} %shard_map.39.rest_1_), channel_id=1, source_target_pairs={{0,1},{1,0},{2,3},{3,2},{4,5},{5,4},{6,7},{7,6},{8,9},{9,8},{10,11... | collective-permute-start | bytes 2359304 | tf_op jit(solution)/shard_map/ppermute | solution.py:18
  43.4 16.4 %collective-permute-start.6 = (f32[4,256,128]{2,1,0:T(8,128)}, f32[4,256,128]{2,1,0:T(8,128)S(1)}, u32[]{:S(2)}, u32[]{:S(2)}) collective-permute-start(f32[4,256,128]{2,1,0:T(8,128)} %get-tuple-element.7.rest_0_), channel_id=1, source_target_pairs={{2,0},{4,2},{6,4},{8,6},{10,8},{12,10},{14,12},{16,14},{18,16},{20... | collective-permute-start | bytes 1572872 | tf_op jit(solution)/shard_map/ppermute | solution.py:24
  45.4 20.7 %collective-permute-start.5 = (f32[4,256,128]{2,1,0:T(8,128)}, f32[4,256,128]{2,1,0:T(8,128)S(1)}, u32[]{:S(2)}, u32[]{:S(2)}) collective-permute-start(f32[4,256,128]{2,1,0:T(8,128)} %get-tuple-element.7.rest_0_), channel_id=1, source_target_pairs={{0,2},{2,4},{4,6},{6,8},{8,10},{10,12},{12,14},{14,16},{16,18},{18... | collective-permute-start | bytes 1572872 | tf_op jit(solution)/shard_map/ppermute | solution.py:23
  49.3 1.7 %collective-permute-start.3 = (f32[3,128,128]{2,1,0:T(8,128)}, f32[3,128,128]{2,1,0:T(8,128)S(1)}, u32[]{:S(2)}, u32[]{:S(2)}) collective-permute-start(f32[3,128,128]{2,1,0:T(8,128)} %get-tuple-element.8), channel_id=1, source_target_pairs={{0,1},{1,0},{2,3},{3,2},{4,5},{5,4},{6,7},{7,6},{8,9},{9,8},{10,11... | collective-permute-start | bytes 589832 | tf_op jit(solution)/shard_map/ppermute | solution.py:18
  51.0 0.7 copy-start.1
  59.9 6.2 %copy-start.3 = (f32[4,256,128]{2,1,0:T(8,128)}, f32[4,256,128]{2,1,0:T(8,128)S(1)}, u32[]{:S(2)}) copy-start(f32[4,256,128]{2,1,0:T(8,128)S(1)} %collective-permute-done.6.rest_5_) | copy-start | bytes 1572868
  66.0 0.8 %copy-start.4 = (f32[4,256,128]{2,1,0:T(8,128)}, f32[4,256,128]{2,1,0:T(8,128)S(1)}, u32[]{:S(2)}) copy-start(f32[4,256,128]{2,1,0:T(8,128)S(1)} %collective-permute-done.5.rest_4_) | copy-start | bytes 1572868
  66.8 0.9 %copy-start.2 = (f32[6,256,128]{2,1,0:T(8,128)}, f32[6,256,128]{2,1,0:T(8,128)S(1)}, u32[]{:S(2)}) copy-start(f32[6,256,128]{2,1,0:T(8,128)S(1)} %collective-permute-done.4.rest_3_) | copy-start | bytes 2359300
where the time goes:
time: 73.1 us; the launch traced here: 72.8 us
  waiting for transfers between devices  29.9 us (41%)
  Pallas kernels  20.3 us (28%)
  starting transfers between devices  18.3 us (25%)
  local copies, waits for them, and re-layouts  4.21 us (6%)
    pallas_call x4, Pallas kernels, band_call(): pl.pallas_call(functools.partial(band_kernel, tiles, odd, len(mine), scal...  18.1 us
    ppermute x2, waiting for transfers between devices, send_block(): lax.ppermute(block, 'rows', [(i, i + 1) for i in range(count - 1)])  14.4 us
    ppermute x2, waiting for transfers between devices, send_block(): lax.ppermute(block, 'rows', [(i + 1, i) for i in range(count - 1)])  13.9 us
    ppermute x2, starting transfers between devices, send_block(): lax.ppermute(block, 'rows', [(i + 1, i) for i in range(count - 1)])  12.4 us
    ppermute x2, starting transfers between devices, send_block(): lax.ppermute(block, 'rows', [(i, i + 1) for i in range(count - 1)])  5.84 us
    unnamed x16, local copies, waits for them, and re-layouts  3.61 us
    pallas_call x1, Pallas kernels, first_block(): pl.pallas_call(block_kernel, out_shape=jax.ShapeDtypeStruct((len(DIAG),)...  2.17 us
    ppermute x3, waiting for transfers between devices, swap_help(): return lax.ppermute(value, 'help', [(0, 1), (1, 0)])  1.64 us
  transfers between devices with their start and end apart: 7, of which 5 were waited for; matrix products, arithmetic and copies ran while one was open for 1% of the time, Pallas kernels for 14%

commit v1 on v0

--- a/solution.py
+++ b/solution.py
@@ -199,18 +199,22 @@
     )(*args)
 
 
-def block_kernel(pattern_ref, density_ref, out_ref):
+def block_kernel(pattern_ref, *refs):
+    out_ref = refs[-1]
     for index, (row, slot) in enumerate(DIAG):
-        out_ref[index] = density_ref[row, slot] * pattern_ref[row, slot].astype(jnp.float32)
+        out_ref[index] = refs[index][0, 0] * pattern_ref[row, slot].astype(jnp.float32)
 
 
 def first_block(pattern, density):
+    tile = (1, 1) + density.shape[2:]
+    specs = [pl.BlockSpec(tile, functools.partial(lambda r, s, i: (r, s, 0, 0), row, slot)) for row, slot in DIAG]
     return pl.pallas_call(
         block_kernel,
+        grid=(1,),
         out_shape=jax.ShapeDtypeStruct((len(DIAG),) + density.shape[2:], jnp.float32),
-        in_specs=[pl.BlockSpec(memory_space=pltpu.SMEM), pl.BlockSpec(memory_space=pltpu.VMEM)],
-        out_specs=pl.BlockSpec(memory_space=pltpu.VMEM),
-    )(pattern, density)
+        in_specs=[pl.BlockSpec(memory_space=pltpu.SMEM)] + specs,
+        out_specs=pl.BlockSpec((len(DIAG),) + density.shape[2:], lambda i: (0, 0, 0)),
+    )(pattern, *([density] * len(DIAG)))
 
 
 def purify(density, pattern, truncation):

time: 73.1 us -> 72.9 us (level)
  no operation moved by 1% of the time
where the time goes in v1:
time: 72.9 us; the launch traced here: 72.6 us
  waiting for transfers between devices  29.9 us (41%)
  Pallas kernels  20.1 us (28%)
  starting transfers between devices  18.3 us (25%)
  local copies, waits for them, and re-layouts  4.21 us (6%)
    pallas_call x4, Pallas kernels, band_call(): pl.pallas_call(functools.partial(band_kernel, tiles, odd, len(mine), scal...  18.1 us
    ppermute x2, waiting for transfers between devices, send_block(): lax.ppermute(block, 'rows', [(i, i + 1) for i in range(count - 1)])  14.4 us
    ppermute x2, waiting for transfers between devices, send_block(): lax.ppermute(block, 'rows', [(i + 1, i) for i in range(count - 1)])  13.9 us
    ppermute x2, starting transfers between devices, send_block(): lax.ppermute(block, 'rows', [(i + 1, i) for i in range(count - 1)])  12.4 us
    ppermute x2, starting transfers between devices, send_block(): lax.ppermute(block, 'rows', [(i, i + 1) for i in range(count - 1)])  5.84 us
    unnamed x16, local copies, waits for them, and re-layouts  3.61 us
    pallas_call x1, Pallas kernels, first_block(): pl.pallas_call(block_kernel, grid=(1,), out_shape=jax.ShapeDtypeStruct((l...  1.94 us
    ppermute x3, waiting for transfers between devices, swap_help(): return lax.ppermute(value, 'help', [(0, 1), (1, 0)])  1.64 us
  transfers between devices with their start and end apart: 7, of which 5 were waited for; matrix products, arithmetic and copies ran while one was open for 1% of the time, Pallas kernels for 14%

profile of v1, /device:TPU:6, one launch (start us, length us, event | category | flops | bytes accessed | tf_op | source)
XLA Modules:
  0.0 72.6 jit_solution(14481165468692309822)
XLA Ops:
  0.0 0.0 copy-start.7
  0.0 0.0 collective-permute-start
  0.0 1.9 %shard_map.38 = f32[4,256,128]{2,1,0:T(8,128)} custom-call(s32[2,5]{1,0:T(2,128)} %scale_ref.7, f32[2,5,256,128]{3,2,1,0:T(8,128)} %rest_0_.3, f32[2,5,256,128]{3,2,1,0:T(8,128)} %rest_0_.3, f32[2,5,256,128]{3,2,1,0:T(8,128)} %rest_0_.3, f32[2,5,256,128]{3,2,1,0:T(8,128)} %rest_0_.3), custom_call_target="tpu_custom_call" | custom-call | tf_op jit(solution)/shard_map/pallas_call | solution.py:211
  1.9 10.5 %collective-permute-start.2 = (f32[4,256,128]{2,1,0:T(8,128)}, f32[4,256,128]{2,1,0:T(8,128)S(1)}, u32[]{:S(2)}, u32[]{:S(2)}) collective-permute-start(f32[4,256,128]{2,1,0:T(8,128)} %shard_map.38), channel_id=1, source_target_pairs={{2,0},{4,2},{6,4},{8,6},{10,8},{12,10},{14,12},{16,14},{18,16},{20... | collective-permute-start | bytes 1572872 | tf_op jit(solution)/shard_map/ppermute | solution.py:24
  12.4 1.9 %collective-permute-start.1 = (f32[4,256,128]{2,1,0:T(8,128)}, f32[4,256,128]{2,1,0:T(8,128)S(1)}, u32[]{:S(2)}, u32[]{:S(2)}) collective-permute-start(f32[4,256,128]{2,1,0:T(8,128)} %shard_map.38), channel_id=1, source_target_pairs={{0,2},{2,4},{4,6},{6,8},{8,10},{10,12},{12,14},{14,16},{16,18},{18... | collective-permute-start | bytes 1572872 | tf_op jit(solution)/shard_map/ppermute | solution.py:23
  14.4 0.0 copy-done.7
  14.4 0.6 slice_bitcast_fusion
  15.0 9.6 %collective-permute-done.2.rest_3_ = f32[4,256,128]{2,1,0:T(8,128)S(1)} collective-permute-done((f32[4,256,128]{2,1,0:T(8,128)}, f32[4,256,128]{2,1,0:T(8,128)S(1)}, u32[]{:S(2)}, u32[]{:S(2)}) %collective-permute-start.2) | collective-permute-done | bytes 524320 | tf_op jit(solution)/shard_map/ppermute | solution.py:24
  24.6 0.0 copy-start.5
  24.6 8.2 %collective-permute-done.1.rest_2_ = f32[4,256,128]{2,1,0:T(8,128)S(1)} collective-permute-done((f32[4,256,128]{2,1,0:T(8,128)}, f32[4,256,128]{2,1,0:T(8,128)S(1)}, u32[]{:S(2)}, u32[]{:S(2)}) %collective-permute-start.1) | collective-permute-done | bytes 524320 | tf_op jit(solution)/shard_map/ppermute | solution.py:23
  32.8 0.0 copy-start.6
  32.8 0.0 collective-permute-done.rest_1_
  32.8 0.0 copy-start
  32.8 0.0 copy-done.5
  32.8 0.8 %copy-done.6 = f32[4,256,128]{2,1,0:T(8,128)} copy-done((f32[4,256,128]{2,1,0:T(8,128)}, f32[4,256,128]{2,1,0:T(8,128)S(1)}, u32[]{:S(2)}) %copy-start.6) | copy-done | bytes 524312
  33.6 0.4 copy-done
  34.0 4.9 %shard_map.39.rest_1_ = f32[6,256,128]{2,1,0:T(8,128)} custom-call(s32[1]{0:T(128)} %bitcast.side_ref, s32[2,5]{1,0:T(2,128)} %scale_ref.7, s32[2,5]{1,0:T(2,128)} %get-tuple-element.9.keep_ref, f32[2,5,256,128]{3,2,1,0:T(8,128)} %rest_0_.3, f32[2,5,256,128]{3,2,1,0:T(8,128)} %copy-done, f32[4,256,128]{2,1,0:T(8,128)} %copy-done.6, f32[4,256,128]{2,1,0:T(8,128)} %copy-done.5), custom_call_target="tpu_custom_call" | custom-call | tf_op jit(solution)/shard_map/pallas_call | solution.py:193
  38.9 0.0 collective-permute-start.4
  38.9 4.3 %shard_map.37 = (f32[4,256,128]{2,1,0:T(8,128)}, f32[3,128,128]{2,1,0:T(8,128)}) custom-call(s32[1]{0:T(128)} %bitcast.side_ref, s32[2,5]{1,0:T(2,128)} %scale_ref.7, s32[2,5]{1,0:T(2,128)} %get-tuple-element.9.keep_ref, f32[2,5,256,128]{3,2,1,0:T(8,128)} %rest_0_.3, f32[2,5,256,128]{3,2,1,0:T(8,128)} %copy-done), custom_call_target="tpu_custom_call" | custom-call | tf_op jit(solution)/shard_map/pallas_call | solution.py:193
  43.2 1.9 %collective-permute-start.6 = (f32[4,256,128]{2,1,0:T(8,128)}, f32[4,256,128]{2,1,0:T(8,128)S(1)}, u32[]{:S(2)}, u32[]{:S(2)}) collective-permute-start(f32[4,256,128]{2,1,0:T(8,128)} %get-tuple-element.7.rest_0_), channel_id=1, source_target_pairs={{2,0},{4,2},{6,4},{8,6},{10,8},{12,10},{14,12},{16,14},{18,16},{20... | collective-permute-start | bytes 1572872 | tf_op jit(solution)/shard_map/ppermute | solution.py:24
  45.1 3.9 %collective-permute-start.5 = (f32[4,256,128]{2,1,0:T(8,128)}, f32[4,256,128]{2,1,0:T(8,128)S(1)}, u32[]{:S(2)}, u32[]{:S(2)}) collective-permute-start(f32[4,256,128]{2,1,0:T(8,128)} %get-tuple-element.7.rest_0_), channel_id=1, source_target_pairs={{0,2},{2,4},{4,6},{6,8},{8,10},{10,12},{12,14},{14,16},{16,18},{18... | collective-permute-start | bytes 1572872 | tf_op jit(solution)/shard_map/ppermute | solution.py:23
  49.1 0.1 collective-permute-start.3
  49.2 1.6 %collective-permute-done.3.rest_2_ = f32[3,128,128]{2,1,0:T(8,128)S(1)} collective-permute-done((f32[3,128,128]{2,1,0:T(8,128)}, f32[3,128,128]{2,1,0:T(8,128)S(1)}, u32[]{:S(2)}, u32[]{:S(2)}) %collective-permute-start.3) | collective-permute-done | bytes 196640 | tf_op jit(solution)/shard_map/ppermute | solution.py:18
  50.8 0.7 copy-done.1
  51.5 3.8 %shard_map.40.rest_6_ = f32[2,5,256,128]{3,2,1,0:T(8,128)} custom-call(s32[1]{0:T(128)} %bitcast.side_ref, s32[2,5]{1,0:T(2,128)} %scale_ref.7, s32[2,5]{1,0:T(2,128)} %get-tuple-element.10.keep_ref, f32[4,256,128]{2,1,0:T(8,128)} %get-tuple-element.7.rest_0_, f32[6,256,128]{2,1,0:T(8,128)} %shard_map.39.rest_1_, f32[3,128,128]{2,1,0:T(8,128)} %copy-done.1), custom_call_target="tpu_custom_call" | custom-call | tf_op jit(solution)/shard_map/pallas_call | solution.py:193
  55.3 4.3 %collective-permute-done.6.rest_5_ = f32[4,256,128]{2,1,0:T(8,128)S(1)} collective-permute-done((f32[4,256,128]{2,1,0:T(8,128)}, f32[4,256,128]{2,1,0:T(8,128)S(1)}, u32[]{:S(2)}, u32[]{:S(2)}) %collective-permute-start.6) | collective-permute-done | bytes 524320 | tf_op jit(solution)/shard_map/ppermute | solution.py:24
  59.6 6.1 %collective-permute-done.5.rest_4_ = f32[4,256,128]{2,1,0:T(8,128)S(1)} collective-permute-done((f32[4,256,128]{2,1,0:T(8,128)}, f32[4,256,128]{2,1,0:T(8,128)S(1)}, u32[]{:S(2)}, u32[]{:S(2)}) %collective-permute-start.5) | collective-permute-done | bytes 524320 | tf_op jit(solution)/shard_map/ppermute | solution.py:23
  65.8 0.0 collective-permute-done.4.rest_3_
  65.8 0.0 copy-done.3
  65.8 0.8 %copy-done.4 = f32[4,256,128]{2,1,0:T(8,128)} copy-done((f32[4,256,128]{2,1,0:T(8,128)}, f32[4,256,128]{2,1,0:T(8,128)S(1)}, u32[]{:S(2)}) %copy-start.4) | copy-done | bytes 524312
  66.6 0.9 %copy-done.2 = f32[6,256,128]{2,1,0:T(8,128)} copy-done((f32[6,256,128]{2,1,0:T(8,128)}, f32[6,256,128]{2,1,0:T(8,128)S(1)}, u32[]{:S(2)}) %copy-start.2) | copy-done | bytes 786456
  67.5 5.1 %shard_map.41 = f32[2,5,256,128]{3,2,1,0:T(8,128)} custom-call(s32[1]{0:T(128)} %bitcast.side_ref, s32[2,5]{1,0:T(2,128)} %scale_ref.7, s32[2,5]{1,0:T(2,128)} %get-tuple-element.10.keep_ref, f32[4,256,128]{2,1,0:T(8,128)} %get-tuple-element.7.rest_0_, f32[6,256,128]{2,1,0:T(8,128)} %shard_map.39.rest_1_, f32[3,128,128]{2,1,0:T(8,128)} %copy-done.1, ...), custom_call_target="tpu_custom_call" | custom-call | tf_op jit(solution)/shard_map/pallas_call | solution.py:193
  (4 shorter events, 0.0 us)
Async XLA Ops:
  0.0 14.4 %copy-start.7 = (s32[2,2,5]{2,1,0:T(2,128)S(1)}, s32[2,2,5]{2,1,0:T(2,128)}, u32[]{:S(2)}) copy-start(s32[2,2,5]{2,1,0:T(2,128)} %param.5) | copy-start | bytes 244
  0.0 32.8 %collective-permute-start = (f32[2,5,256,128]{3,2,1,0:T(8,128)}, f32[2,5,256,128]{3,2,1,0:T(8,128)S(1)}, u32[]{:S(2)}, u32[]{:S(2)}) collective-permute-start(f32[2,5,256,128]{3,2,1,0:T(8,128)} %rest_0_.3), channel_id=1, source_target_pairs={{0,1},{1,0},{2,3},{3,2},{4,5},{5,4},{6,7},{7,6},{8,9},{9,8},{10,11... | collective-permute-start | bytes 3932168 | tf_op jit(solution)/shard_map/ppermute | solution.py:18
  1.9 22.6 %collective-permute-start.2 = (f32[4,256,128]{2,1,0:T(8,128)}, f32[4,256,128]{2,1,0:T(8,128)S(1)}, u32[]{:S(2)}, u32[]{:S(2)}) collective-permute-start(f32[4,256,128]{2,1,0:T(8,128)} %shard_map.38), channel_id=1, source_target_pairs={{2,0},{4,2},{6,4},{8,6},{10,8},{12,10},{14,12},{16,14},{18,16},{20... | collective-permute-start | bytes 1572872 | tf_op jit(solution)/shard_map/ppermute | solution.py:24
  12.4 20.4 %collective-permute-start.1 = (f32[4,256,128]{2,1,0:T(8,128)}, f32[4,256,128]{2,1,0:T(8,128)S(1)}, u32[]{:S(2)}, u32[]{:S(2)}) collective-permute-start(f32[4,256,128]{2,1,0:T(8,128)} %shard_map.38), channel_id=1, source_target_pairs={{0,2},{2,4},{4,6},{6,8},{8,10},{10,12},{12,14},{14,16},{16,18},{18... | collective-permute-start | bytes 1572872 | tf_op jit(solution)/shard_map/ppermute | solution.py:23
  24.6 8.2 %copy-start.5 = (f32[4,256,128]{2,1,0:T(8,128)}, f32[4,256,128]{2,1,0:T(8,128)S(1)}, u32[]{:S(2)}) copy-start(f32[4,256,128]{2,1,0:T(8,128)S(1)} %collective-permute-done.2.rest_3_) | copy-start | bytes 1572868
  32.8 0.8 %copy-start.6 = (f32[4,256,128]{2,1,0:T(8,128)}, f32[4,256,128]{2,1,0:T(8,128)S(1)}, u32[]{:S(2)}) copy-start(f32[4,256,128]{2,1,0:T(8,128)S(1)} %collective-permute-done.1.rest_2_) | copy-start | bytes 1572868
  32.8 1.2 %copy-start = (f32[2,5,256,128]{3,2,1,0:T(8,128)}, f32[2,5,256,128]{3,2,1,0:T(8,128)S(1)}, u32[]{:S(2)}) copy-start(f32[2,5,256,128]{3,2,1,0:T(8,128)S(1)} %collective-permute-done.rest_1_) | copy-start | bytes 3932164
  38.9 26.9 %collective-permute-start.4 = (f32[6,256,128]{2,1,0:T(8,128)}, f32[6,256,128]{2,1,0:T(8,128)S(1)}, u32[]{:S(2)}, u32[]{:S(2)}) collective-permute-start(f32[6,256,128]{2,1,0:T(8,128)} %shard_map.39.rest_1_), channel_id=1, source_target_pairs={{0,1},{1,0},{2,3},{3,2},{4,5},{5,4},{6,7},{7,6},{8,9},{9,8},{10,11... | collective-permute-start | bytes 2359304 | tf_op jit(solution)/shard_map/ppermute | solution.py:18
  43.2 16.4 %collective-permute-start.6 = (f32[4,256,128]{2,1,0:T(8,128)}, f32[4,256,128]{2,1,0:T(8,128)S(1)}, u32[]{:S(2)}, u32[]{:S(2)}) collective-permute-start(f32[4,256,128]{2,1,0:T(8,128)} %get-tuple-element.7.rest_0_), channel_id=1, source_target_pairs={{2,0},{4,2},{6,4},{8,6},{10,8},{12,10},{14,12},{16,14},{18,16},{20... | collective-permute-start | bytes 1572872 | tf_op jit(solution)/shard_map/ppermute | solution.py:24
  45.1 20.7 %collective-permute-start.5 = (f32[4,256,128]{2,1,0:T(8,128)}, f32[4,256,128]{2,1,0:T(8,128)S(1)}, u32[]{:S(2)}, u32[]{:S(2)}) collective-permute-start(f32[4,256,128]{2,1,0:T(8,128)} %get-tuple-element.7.rest_0_), channel_id=1, source_target_pairs={{0,2},{2,4},{4,6},{6,8},{8,10},{10,12},{12,14},{14,16},{16,18},{18... | collective-permute-start | bytes 1572872 | tf_op jit(solution)/shard_map/ppermute | solution.py:23
  49.1 1.7 %collective-permute-start.3 = (f32[3,128,128]{2,1,0:T(8,128)}, f32[3,128,128]{2,1,0:T(8,128)S(1)}, u32[]{:S(2)}, u32[]{:S(2)}) collective-permute-start(f32[3,128,128]{2,1,0:T(8,128)} %get-tuple-element.8), channel_id=1, source_target_pairs={{0,1},{1,0},{2,3},{3,2},{4,5},{5,4},{6,7},{7,6},{8,9},{9,8},{10,11... | collective-permute-start | bytes 589832 | tf_op jit(solution)/shard_map/ppermute | solution.py:18
  50.8 0.7 copy-start.1
  59.6 6.2 %copy-start.3 = (f32[4,256,128]{2,1,0:T(8,128)}, f32[4,256,128]{2,1,0:T(8,128)S(1)}, u32[]{:S(2)}) copy-start(f32[4,256,128]{2,1,0:T(8,128)S(1)} %collective-permute-done.6.rest_5_) | copy-start | bytes 1572868
  65.8 0.8 %copy-start.4 = (f32[4,256,128]{2,1,0:T(8,128)}, f32[4,256,128]{2,1,0:T(8,128)S(1)}, u32[]{:S(2)}) copy-start(f32[4,256,128]{2,1,0:T(8,128)S(1)} %collective-permute-done.5.rest_4_) | copy-start | bytes 1572868
  66.6 0.9 %copy-start.2 = (f32[6,256,128]{2,1,0:T(8,128)}, f32[6,256,128]{2,1,0:T(8,128)S(1)}, u32[]{:S(2)}) copy-start(f32[6,256,128]{2,1,0:T(8,128)S(1)} %collective-permute-done.4.rest_3_) | copy-start | bytes 2359300

commit v2 on v1

--- a/solution.py
+++ b/solution.py
@@ -114,6 +114,11 @@
                 col = row + slot - 2
                 where = (row, slice(place_k * tile, (place_k + 1) * tile), slice(place * half, (place + 1) * half))
                 if abs(k - col) > 2:
+                    first = place - place % 2
+                    chunk = range(first, min(first + 2, len(by_row[row])))
+                    used = [p for p, o in enumerate(offsets) if any(abs(o - by_row[row][q][1]) <= 2 for q in chunk)]
+                    if not used[0] <= place_k <= used[-1]:
+                        continue
                     rh_ref[where] = jnp.zeros((tile, half), jnp.bfloat16)
                     rl_ref[where] = jnp.zeros((tile, half), jnp.bfloat16)
                     continue

time: 72.9 us -> 72.9 us (level)
  no operation moved by 1% of the time
where the time goes in v2:
time: 72.9 us; the launch traced here: 72.6 us
  waiting for transfers between devices  29.9 us (41%)
  Pallas kernels  20.1 us (28%)
  starting transfers between devices  18.3 us (25%)
  local copies, waits for them, and re-layouts  4.21 us (6%)
    pallas_call x4, Pallas kernels, band_call(): pl.pallas_call(functools.partial(band_kernel, tiles, odd, len(mine), scal...  18.1 us
    ppermute x2, waiting for transfers between devices, send_block(): lax.ppermute(block, 'rows', [(i, i + 1) for i in range(count - 1)])  14.4 us
    ppermute x2, waiting for transfers between devices, send_block(): lax.ppermute(block, 'rows', [(i + 1, i) for i in range(count - 1)])  13.9 us
    ppermute x2, starting transfers between devices, send_block(): lax.ppermute(block, 'rows', [(i + 1, i) for i in range(count - 1)])  12.4 us
    ppermute x2, starting transfers between devices, send_block(): lax.ppermute(block, 'rows', [(i, i + 1) for i in range(count - 1)])  5.84 us
    unnamed x16, local copies, waits for them, and re-layouts  3.61 us
    pallas_call x1, Pallas kernels, first_block(): pl.pallas_call(block_kernel, grid=(1,), out_shape=jax.ShapeDtypeStruct((l...  1.94 us
    ppermute x3, waiting for transfers between devices, swap_help(): return lax.ppermute(value, 'help', [(0, 1), (1, 0)])  1.64 us
  transfers between devices with their start and end apart: 7, of which 5 were waited for; matrix products, arithmetic and copies ran while one was open for 1% of the time, Pallas kernels for 14%

profile of v2, /device:TPU:6, one launch (start us, length us, event | category | flops | bytes accessed | tf_op | source)
XLA Modules:
  0.0 72.6 jit_solution(1561531469911781803)
XLA Ops:
  0.0 0.0 copy-start.7
  0.0 0.0 collective-permute-start
  0.0 1.9 %shard_map.38 = f32[4,256,128]{2,1,0:T(8,128)} custom-call(s32[2,5]{1,0:T(2,128)} %scale_ref.7, f32[2,5,256,128]{3,2,1,0:T(8,128)} %rest_0_.3, f32[2,5,256,128]{3,2,1,0:T(8,128)} %rest_0_.3, f32[2,5,256,128]{3,2,1,0:T(8,128)} %rest_0_.3, f32[2,5,256,128]{3,2,1,0:T(8,128)} %rest_0_.3), custom_call_target="tpu_custom_call" | custom-call | tf_op jit(solution)/shard_map/pallas_call | solution.py:216
  1.9 10.5 %collective-permute-start.2 = (f32[4,256,128]{2,1,0:T(8,128)}, f32[4,256,128]{2,1,0:T(8,128)S(1)}, u32[]{:S(2)}, u32[]{:S(2)}) collective-permute-start(f32[4,256,128]{2,1,0:T(8,128)} %shard_map.38), channel_id=1, source_target_pairs={{2,0},{4,2},{6,4},{8,6},{10,8},{12,10},{14,12},{16,14},{18,16},{20... | collective-permute-start | bytes 1572872 | tf_op jit(solution)/shard_map/ppermute | solution.py:24
  12.4 1.9 %collective-permute-start.1 = (f32[4,256,128]{2,1,0:T(8,128)}, f32[4,256,128]{2,1,0:T(8,128)S(1)}, u32[]{:S(2)}, u32[]{:S(2)}) collective-permute-start(f32[4,256,128]{2,1,0:T(8,128)} %shard_map.38), channel_id=1, source_target_pairs={{0,2},{2,4},{4,6},{6,8},{8,10},{10,12},{12,14},{14,16},{16,18},{18... | collective-permute-start | bytes 1572872 | tf_op jit(solution)/shard_map/ppermute | solution.py:23
  14.4 0.0 copy-done.7
  14.4 0.6 slice_bitcast_fusion
  15.0 9.6 %collective-permute-done.2.rest_3_ = f32[4,256,128]{2,1,0:T(8,128)S(1)} collective-permute-done((f32[4,256,128]{2,1,0:T(8,128)}, f32[4,256,128]{2,1,0:T(8,128)S(1)}, u32[]{:S(2)}, u32[]{:S(2)}) %collective-permute-start.2) | collective-permute-done | bytes 524320 | tf_op jit(solution)/shard_map/ppermute | solution.py:24
  24.6 0.0 copy-start.5
  24.6 8.2 %collective-permute-done.1.rest_2_ = f32[4,256,128]{2,1,0:T(8,128)S(1)} collective-permute-done((f32[4,256,128]{2,1,0:T(8,128)}, f32[4,256,128]{2,1,0:T(8,128)S(1)}, u32[]{:S(2)}, u32[]{:S(2)}) %collective-permute-start.1) | collective-permute-done | bytes 524320 | tf_op jit(solution)/shard_map/ppermute | solution.py:23
  32.8 0.0 copy-start.6
  32.8 0.0 collective-permute-done.rest_1_
  32.8 0.0 copy-start
  32.8 0.0 copy-done.5
  32.8 0.8 %copy-done.6 = f32[4,256,128]{2,1,0:T(8,128)} copy-done((f32[4,256,128]{2,1,0:T(8,128)}, f32[4,256,128]{2,1,0:T(8,128)S(1)}, u32[]{:S(2)}) %copy-start.6) | copy-done | bytes 524312
  33.6 0.4 copy-done
  34.0 4.9 %shard_map.39.rest_1_ = f32[6,256,128]{2,1,0:T(8,128)} custom-call(s32[1]{0:T(128)} %bitcast.side_ref, s32[2,5]{1,0:T(2,128)} %scale_ref.7, s32[2,5]{1,0:T(2,128)} %get-tuple-element.9.keep_ref, f32[2,5,256,128]{3,2,1,0:T(8,128)} %rest_0_.3, f32[2,5,256,128]{3,2,1,0:T(8,128)} %copy-done, f32[4,256,128]{2,1,0:T(8,128)} %copy-done.6, f32[4,256,128]{2,1,0:T(8,128)} %copy-done.5), custom_call_target="tpu_custom_call" | custom-call | tf_op jit(solution)/shard_map/pallas_call | solution.py:198
  38.9 0.0 collective-permute-start.4
  38.9 4.3 %shard_map.37 = (f32[4,256,128]{2,1,0:T(8,128)}, f32[3,128,128]{2,1,0:T(8,128)}) custom-call(s32[1]{0:T(128)} %bitcast.side_ref, s32[2,5]{1,0:T(2,128)} %scale_ref.7, s32[2,5]{1,0:T(2,128)} %get-tuple-element.9.keep_ref, f32[2,5,256,128]{3,2,1,0:T(8,128)} %rest_0_.3, f32[2,5,256,128]{3,2,1,0:T(8,128)} %copy-done), custom_call_target="tpu_custom_call" | custom-call | tf_op jit(solution)/shard_map/pallas_call | solution.py:198
  43.2 1.9 %collective-permute-start.6 = (f32[4,256,128]{2,1,0:T(8,128)}, f32[4,256,128]{2,1,0:T(8,128)S(1)}, u32[]{:S(2)}, u32[]{:S(2)}) collective-permute-start(f32[4,256,128]{2,1,0:T(8,128)} %get-tuple-element.7.rest_0_), channel_id=1, source_target_pairs={{2,0},{4,2},{6,4},{8,6},{10,8},{12,10},{14,12},{16,14},{18,16},{20... | collective-permute-start | bytes 1572872 | tf_op jit(solution)/shard_map/ppermute | solution.py:24
  45.1 3.9 %collective-permute-start.5 = (f32[4,256,128]{2,1,0:T(8,128)}, f32[4,256,128]{2,1,0:T(8,128)S(1)}, u32[]{:S(2)}, u32[]{:S(2)}) collective-permute-start(f32[4,256,128]{2,1,0:T(8,128)} %get-tuple-element.7.rest_0_), channel_id=1, source_target_pairs={{0,2},{2,4},{4,6},{6,8},{8,10},{10,12},{12,14},{14,16},{16,18},{18... | collective-permute-start | bytes 1572872 | tf_op jit(solution)/shard_map/ppermute | solution.py:23
  49.1 0.1 collective-permute-start.3
  49.2 1.6 %collective-permute-done.3.rest_2_ = f32[3,128,128]{2,1,0:T(8,128)S(1)} collective-permute-done((f32[3,128,128]{2,1,0:T(8,128)}, f32[3,128,128]{2,1,0:T(8,128)S(1)}, u32[]{:S(2)}, u32[]{:S(2)}) %collective-permute-start.3) | collective-permute-done | bytes 196640 | tf_op jit(solution)/shard_map/ppermute | solution.py:18
  50.8 0.7 copy-done.1
  51.5 3.8 %shard_map.40.rest_6_ = f32[2,5,256,128]{3,2,1,0:T(8,128)} custom-call(s32[1]{0:T(128)} %bitcast.side_ref, s32[2,5]{1,0:T(2,128)} %scale_ref.7, s32[2,5]{1,0:T(2,128)} %get-tuple-element.10.keep_ref, f32[4,256,128]{2,1,0:T(8,128)} %get-tuple-element.7.rest_0_, f32[6,256,128]{2,1,0:T(8,128)} %shard_map.39.rest_1_, f32[3,128,128]{2,1,0:T(8,128)} %copy-done.1), custom_call_target="tpu_custom_call" | custom-call | tf_op jit(solution)/shard_map/pallas_call | solution.py:198
  55.3 4.3 %collective-permute-done.6.rest_5_ = f32[4,256,128]{2,1,0:T(8,128)S(1)} collective-permute-done((f32[4,256,128]{2,1,0:T(8,128)}, f32[4,256,128]{2,1,0:T(8,128)S(1)}, u32[]{:S(2)}, u32[]{:S(2)}) %collective-permute-start.6) | collective-permute-done | bytes 524320 | tf_op jit(solution)/shard_map/ppermute | solution.py:24
  59.6 6.1 %collective-permute-done.5.rest_4_ = f32[4,256,128]{2,1,0:T(8,128)S(1)} collective-permute-done((f32[4,256,128]{2,1,0:T(8,128)}, f32[4,256,128]{2,1,0:T(8,128)S(1)}, u32[]{:S(2)}, u32[]{:S(2)}) %collective-permute-start.5) | collective-permute-done | bytes 524320 | tf_op jit(solution)/shard_map/ppermute | solution.py:23
  65.8 0.0 collective-permute-done.4.rest_3_
  65.8 0.0 copy-done.3
  65.8 0.8 %copy-done.4 = f32[4,256,128]{2,1,0:T(8,128)} copy-done((f32[4,256,128]{2,1,0:T(8,128)}, f32[4,256,128]{2,1,0:T(8,128)S(1)}, u32[]{:S(2)}) %copy-start.4) | copy-done | bytes 524312
  66.6 0.9 %copy-done.2 = f32[6,256,128]{2,1,0:T(8,128)} copy-done((f32[6,256,128]{2,1,0:T(8,128)}, f32[6,256,128]{2,1,0:T(8,128)S(1)}, u32[]{:S(2)}) %copy-start.2) | copy-done | bytes 786456
  67.5 5.1 %shard_map.41 = f32[2,5,256,128]{3,2,1,0:T(8,128)} custom-call(s32[1]{0:T(128)} %bitcast.side_ref, s32[2,5]{1,0:T(2,128)} %scale_ref.7, s32[2,5]{1,0:T(2,128)} %get-tuple-element.10.keep_ref, f32[4,256,128]{2,1,0:T(8,128)} %get-tuple-element.7.rest_0_, f32[6,256,128]{2,1,0:T(8,128)} %shard_map.39.rest_1_, f32[3,128,128]{2,1,0:T(8,128)} %copy-done.1, ...), custom_call_target="tpu_custom_call" | custom-call | tf_op jit(solution)/shard_map/pallas_call | solution.py:198
  (4 shorter events, 0.0 us)
Async XLA Ops:
  0.0 14.4 %copy-start.7 = (s32[2,2,5]{2,1,0:T(2,128)S(1)}, s32[2,2,5]{2,1,0:T(2,128)}, u32[]{:S(2)}) copy-start(s32[2,2,5]{2,1,0:T(2,128)} %param.5) | copy-start | bytes 244
  0.0 32.8 %collective-permute-start = (f32[2,5,256,128]{3,2,1,0:T(8,128)}, f32[2,5,256,128]{3,2,1,0:T(8,128)S(1)}, u32[]{:S(2)}, u32[]{:S(2)}) collective-permute-start(f32[2,5,256,128]{3,2,1,0:T(8,128)} %rest_0_.3), channel_id=1, source_target_pairs={{0,1},{1,0},{2,3},{3,2},{4,5},{5,4},{6,7},{7,6},{8,9},{9,8},{10,11... | collective-permute-start | bytes 3932168 | tf_op jit(solution)/shard_map/ppermute | solution.py:18
  1.9 22.6 %collective-permute-start.2 = (f32[4,256,128]{2,1,0:T(8,128)}, f32[4,256,128]{2,1,0:T(8,128)S(1)}, u32[]{:S(2)}, u32[]{:S(2)}) collective-permute-start(f32[4,256,128]{2,1,0:T(8,128)} %shard_map.38), channel_id=1, source_target_pairs={{2,0},{4,2},{6,4},{8,6},{10,8},{12,10},{14,12},{16,14},{18,16},{20... | collective-permute-start | bytes 1572872 | tf_op jit(solution)/shard_map/ppermute | solution.py:24
  12.4 20.4 %collective-permute-start.1 = (f32[4,256,128]{2,1,0:T(8,128)}, f32[4,256,128]{2,1,0:T(8,128)S(1)}, u32[]{:S(2)}, u32[]{:S(2)}) collective-permute-start(f32[4,256,128]{2,1,0:T(8,128)} %shard_map.38), channel_id=1, source_target_pairs={{0,2},{2,4},{4,6},{6,8},{8,10},{10,12},{12,14},{14,16},{16,18},{18... | collective-permute-start | bytes 1572872 | tf_op jit(solution)/shard_map/ppermute | solution.py:23
  24.6 8.2 %copy-start.5 = (f32[4,256,128]{2,1,0:T(8,128)}, f32[4,256,128]{2,1,0:T(8,128)S(1)}, u32[]{:S(2)}) copy-start(f32[4,256,128]{2,1,0:T(8,128)S(1)} %collective-permute-done.2.rest_3_) | copy-start | bytes 1572868
  32.8 0.8 %copy-start.6 = (f32[4,256,128]{2,1,0:T(8,128)}, f32[4,256,128]{2,1,0:T(8,128)S(1)}, u32[]{:S(2)}) copy-start(f32[4,256,128]{2,1,0:T(8,128)S(1)} %collective-permute-done.1.rest_2_) | copy-start | bytes 1572868
  32.8 1.2 %copy-start = (f32[2,5,256,128]{3,2,1,0:T(8,128)}, f32[2,5,256,128]{3,2,1,0:T(8,128)S(1)}, u32[]{:S(2)}) copy-start(f32[2,5,256,128]{3,2,1,0:T(8,128)S(1)} %collective-permute-done.rest_1_) | copy-start | bytes 3932164
  38.9 26.9 %collective-permute-start.4 = (f32[6,256,128]{2,1,0:T(8,128)}, f32[6,256,128]{2,1,0:T(8,128)S(1)}, u32[]{:S(2)}, u32[]{:S(2)}) collective-permute-start(f32[6,256,128]{2,1,0:T(8,128)} %shard_map.39.rest_1_), channel_id=1, source_target_pairs={{0,1},{1,0},{2,3},{3,2},{4,5},{5,4},{6,7},{7,6},{8,9},{9,8},{10,11... | collective-permute-start | bytes 2359304 | tf_op jit(solution)/shard_map/ppermute | solution.py:18
  43.2 16.4 %collective-permute-start.6 = (f32[4,256,128]{2,1,0:T(8,128)}, f32[4,256,128]{2,1,0:T(8,128)S(1)}, u32[]{:S(2)}, u32[]{:S(2)}) collective-permute-start(f32[4,256,128]{2,1,0:T(8,128)} %get-tuple-element.7.rest_0_), channel_id=1, source_target_pairs={{2,0},{4,2},{6,4},{8,6},{10,8},{12,10},{14,12},{16,14},{18,16},{20... | collective-permute-start | bytes 1572872 | tf_op jit(solution)/shard_map/ppermute | solution.py:24
  45.1 20.7 %collective-permute-start.5 = (f32[4,256,128]{2,1,0:T(8,128)}, f32[4,256,128]{2,1,0:T(8,128)S(1)}, u32[]{:S(2)}, u32[]{:S(2)}) collective-permute-start(f32[4,256,128]{2,1,0:T(8,128)} %get-tuple-element.7.rest_0_), channel_id=1, source_target_pairs={{0,2},{2,4},{4,6},{6,8},{8,10},{10,12},{12,14},{14,16},{16,18},{18... | collective-permute-start | bytes 1572872 | tf_op jit(solution)/shard_map/ppermute | solution.py:23
  49.1 1.7 %collective-permute-start.3 = (f32[3,128,128]{2,1,0:T(8,128)}, f32[3,128,128]{2,1,0:T(8,128)S(1)}, u32[]{:S(2)}, u32[]{:S(2)}) collective-permute-start(f32[3,128,128]{2,1,0:T(8,128)} %get-tuple-element.8), channel_id=1, source_target_pairs={{0,1},{1,0},{2,3},{3,2},{4,5},{5,4},{6,7},{7,6},{8,9},{9,8},{10,11... | collective-permute-start | bytes 589832 | tf_op jit(solution)/shard_map/ppermute | solution.py:18
  50.8 0.7 copy-start.1
  59.6 6.2 %copy-start.3 = (f32[4,256,128]{2,1,0:T(8,128)}, f32[4,256,128]{2,1,0:T(8,128)S(1)}, u32[]{:S(2)}) copy-start(f32[4,256,128]{2,1,0:T(8,128)S(1)} %collective-permute-done.6.rest_5_) | copy-start | bytes 1572868
  65.8 0.8 %copy-start.4 = (f32[4,256,128]{2,1,0:T(8,128)}, f32[4,256,128]{2,1,0:T(8,128)S(1)}, u32[]{:S(2)}) copy-start(f32[4,256,128]{2,1,0:T(8,128)S(1)} %collective-permute-done.5.rest_4_) | copy-start | bytes 1572868
  66.6 0.9 %copy-start.2 = (f32[6,256,128]{2,1,0:T(8,128)}, f32[6,256,128]{2,1,0:T(8,128)S(1)}, u32[]{:S(2)}) copy-start(f32[6,256,128]{2,1,0:T(8,128)S(1)} %collective-permute-done.4.rest_3_) | copy-start | bytes 2359300
